TPU v7x, 128 devices: a whole 4x4x4 slice. The times are simulated.
128 devices in a mesh: ang: 64 (over x, y_lo, z, core), pix: 2 (over y_hi).
Axes of the slice: x: 4, y: 4 (y_hi: 2, y_lo: 2; y = y_hi * 2 + y_lo), z: 4, core: 2. Of those that a mesh axis runs over, the one named last changes fastest.
Arguments:
- grads: bfloat16 [2, 4096, 128, 512], P(None, 'ang', 'pix')
- circle_pos: int32 [4096], replicated, may hold values from 0 to 4095, as said below
- harmonics: int32 [256], replicated, may hold values from 0 to 4095, as said below
- support: int32 [128, 512], replicated, may hold values 0 or 1
Outputs:
- update: bfloat16 [2, 4096, 128, 512], P(None, 'ang', 'pix')
- harmonic_rms: float32 [256], replicated
Inputs may be any that keep to these rules, and one draw needn't show every extreme that they name: `circle_pos`: the stored angles form 64 aligned blocks of 64 rows; block b holds the circle positions r_b + 64 * j for j = 0 to 63 in this order, and the 64 values r_b are distinct. `harmonics`: 256 distinct harmonic numbers, among them 0 and 4095.
All inputs are finite; a program needn't handle non-finite values.
Results may differ from a plain program's by a relative error of at most 0.015.
Values may be sent and summed in bfloat16 or wider, within the bound.
No kernel may reach another device: no remote copies, remote signals or barrier semaphores. Data moves between devices by JAX's collectives and lax.ppermute only.
A program may use at most 192 MiB of HBM per device.

v0:
```python
import math
import jax
import jax.numpy as jnp
from jax import lax
from jax.sharding import PartitionSpec as P


def phase_pair(product, modulus):
    radians = (product % modulus).astype(jnp.float32) * (2.0 * math.pi / modulus)
    return (jnp.cos(radians), jnp.sin(radians))


def split_parts(value):
    if value.dtype == jnp.bfloat16:
        return (value,)
    high = value.astype(jnp.bfloat16)
    low = (value - high.astype(jnp.float32)).astype(jnp.bfloat16)
    return (high, low)


def split_einsum(form, left, right):
    left_parts = split_parts(left)
    right_parts = split_parts(right)
    total = None
    for left_rank, left_piece in enumerate(left_parts):
        for right_rank, right_piece in enumerate(right_parts):
            if left_rank + right_rank <= 1:
                term = jnp.einsum(form, left_piece, right_piece, preferred_element_type=jnp.float32)
                total = term if total is None else total + term
    return total


def normalize(coef_re, coef_im, weight, cell_count):
    square_sums = jnp.sum(weight[None, :] * (coef_re * coef_re + coef_im * coef_im), axis=1)
    totals = lax.psum(square_sums, ("ang", "pix"))
    harmonic_rms = jnp.sqrt(totals / cell_count + 1e-06)
    factor = weight[None, :] / harmonic_rms[:, None]
    return (coef_re * factor, coef_im * factor, harmonic_rms)


def direct_path(grads, circle_pos, harmonics, weight, cell_count):
    angle_count = circle_pos.shape[0]
    kept_count = harmonics.shape[0]
    moved = lax.all_to_all(grads, "ang", split_axis=2, concat_axis=1, tiled=True)
    row_local = moved.shape[2]
    col_count = moved.shape[3]
    flat = moved.reshape(2, angle_count, row_local * col_count)
    pixel_count = flat.shape[2]
    phase_cos, phase_sin = phase_pair(harmonics[:, None] * circle_pos[None, :], angle_count)
    table = jnp.concatenate((phase_cos, phase_sin), 0)
    products = split_einsum("ka,ap->kp", table, jnp.concatenate((flat[0], flat[1]), 1))
    scale = 1.0 / math.sqrt(angle_count)
    coef_re = (products[:kept_count, :pixel_count] + products[kept_count:, pixel_count:]) * scale
    coef_im = (products[:kept_count, pixel_count:] - products[kept_count:, :pixel_count]) * scale
    step_re, step_im, harmonic_rms = normalize(coef_re, coef_im, weight, cell_count)
    right_side = jnp.concatenate(
        (jnp.concatenate((step_re, -step_im), 0), jnp.concatenate((step_im, step_re), 0)), 1
    )
    synthesis = split_einsum("ka,kp->ap", table, right_side)
    scale_back = 1.0 / math.sqrt(kept_count)
    update = jnp.stack((synthesis[:, :pixel_count], synthesis[:, pixel_count:])) * scale_back
    update = update.astype(jnp.bfloat16).reshape(2, angle_count, row_local, col_count)
    return (lax.all_to_all(update, "ang", split_axis=1, concat_axis=2, tiled=True), harmonic_rms)


def body(grads, circle_pos, harmonics, support):
    ang_count = lax.axis_size("ang")
    row_pix = grads.shape[2]
    row_local = row_pix // ang_count
    col_count = grads.shape[3]
    row_start = lax.axis_index("pix") * row_pix + lax.axis_index("ang") * row_local
    weight = (
        lax.dynamic_slice_in_dim(support, row_start, row_local, 0).astype(jnp.float32).reshape(-1)
    )
    cell_count = float(row_pix * lax.axis_size("pix") * col_count)
    update, harmonic_rms = direct_path(grads, circle_pos, harmonics, weight, cell_count)
    return (update, harmonic_rms)


def solution(mesh):
    placed = (P(None, "ang", "pix", None), P(), P(), P())
    return jax.shard_map(
        body,
        mesh=mesh,
        in_specs=placed,
        out_specs=(P(None, "ang", "pix", None), P()),
        check_vma=False,
    )
```

profile of v0, /device:TPU:1, one launch (start us, length us, event | category | flops | bytes accessed | tf_op | source)
XLA Modules:
  0.0 437.9 jit_solution(5942899219189294290)
XLA Ops:
  0.6 11.5 %copy.18 = bf16[2,64,64,512]{3,1,0,2:T(8,128)(2,1)} copy(bf16[2,64,64,512]{3,2,1,0:T(8,128)(2,1)} %param.4) | data formatting | bytes 16777216 | tf_op args[0]
  12.1 0.0 copy-start.6
  12.1 0.0 copy-start.8
  12.1 11.2 %all-to-all-start = ((bf16[2,64,64,512]{3,1,0,2:T(8,128)(2,1)}), bf16[2,64,64,512]{3,1,0,2:T(8,128)(2,1)}, u32[]{:S(2)}, u32[]{:S(2)}) async-start(bf16[2,64,64,512]{3,1,0,2:T(8,128)(2,1)} %copy.18), calls=%async_computation | async-start | bytes 16777216 | tf_op jit(solution)/shard_map/all_to_all | solution.py:44
  23.3 0.7 dynamic-slice_convert_fusion
  24.1 0.0 copy-done.6
  24.1 0.0 copy-done.8
  24.1 18.0 %fusion.8 = (f32[256,4096]{1,0:T(8,128)}, f32[256,4096]{1,0:T(8,128)}) fusion(s32[4096]{0:T(1024)S(1)} %copy-done.6, s32[256]{0:T(256)S(1)} %copy-done.8), kind=kLoop, calls=%fused_computation.23 | loop fusion | flops 14680064 | bytes 8406016 | tf_op jit(solution)/shard_map/cos | solution.py:10
  42.1 84.6 %all-to-all-done = bf16[2,64,64,512]{3,1,0,2:T(8,128)(2,1)} async-done(((bf16[2,64,64,512]{3,1,0,2:T(8,128)(2,1)}), bf16[2,64,64,512]{3,1,0,2:T(8,128)(2,1)}, u32[]{:S(2)}, u32[]{:S(2)}) %all-to-all-start) | async-done | bytes 8388640 | tf_op jit(solution)/shard_map/all_to_all | solution.py:44
  126.7 7.9 %copy.24 = bf16[2,64,64,512]{3,1,2,0:T(8,128)(2,1)} copy(bf16[2,64,64,512]{3,1,0,2:T(8,128)(2,1)} %all-to-all-done) | data formatting | bytes 16777216 | tf_op jit(solution)/shard_map/all_to_all | solution.py:44
  134.6 0.0 copy-start
  134.6 0.0 copy-start.2
  134.6 5.4 %fusion.27 = (bf16[1,64,64,1,512]{4,2,1,3,0:T(8,128)(2,1)S(1)}, bf16[1,64,64,1,512]{4,2,1,3,0:T(8,128)(2,1)}) fusion(bf16[2,64,64,1,512]{4,2,1,3,0:T(8,128)(2,1)} %bitcast.17), kind=kLoop, calls=%fused_computation.41 | loop fusion | bytes 16777216 | tf_op jit(solution)/shard_map/slice | solution.py:51
  140.0 0.0 copy-start.5
  140.0 2.1 copy-done.5
  142.1 0.0 copy-done
  142.1 1.5 copy-done.2
  143.6 8.0 %fusion.2 = f32[512,1024]{1,0:T(8,128)} fusion(bf16[4096,512]{1,0:T(8,128)(2,1)} %bitcast.21, bf16[4096,512]{1,0:T(8,128)(2,1)S(1)} %bitcast.19, f32[256,4096]{1,0:T(8,128)S(1)} %copy-done.2, f32[256,4096]{1,0:T(8,128)S(1)} %copy-done), kind=kOutput, calls=%fused_computation.15 | convolution fusion | flops 4322230272 | bytes 18874368 | tf_op jit(solution)/shard_map/ka,ap->kp/dot_general | solution.py:28
  151.6 8.5 %fusion.9 = f32[512,1024]{1,0:T(8,128)S(1)} fusion(f32[512,1024]{1,0:T(8,128)} %fusion.2, bf16[4096,512]{1,0:T(8,128)(2,1)} %bitcast.22, bf16[4096,512]{1,0:T(8,128)(2,1)} %bitcast.20, f32[256,4096]{1,0:T(8,128)S(1)} %copy-done.2, f32[256,4096]{1,0:T(8,128)S(1)} %copy-done), kind=kOutput, calls=%fused_computation.24 | convolution fusion | flops 4320657408 | bytes 20971520 | tf_op jit(solution)/shard_map/ka,ap->kp/dot_general | solution.py:28
  160.1 0.0 copy-start.4
  160.2 1.3 copy-done.4
  161.5 0.2 multiply_reduce_fusion
  161.7 70.5 %psum.7 = f32[256]{0:T(256)S(1)} all-reduce(f32[256]{0:T(256)S(1)} %multiply_reduce_fusion), channel_id=1, replica_groups=mesh['ang'=64,'pix'=2] {'ang','pix'}, use_global_device_ids=true, to_apply=%region_1.2 | all-reduce | flops 256 | bytes 2048 | tf_op jit(solution)/shard_map/psum | solution.py:35
  232.2 0.0 copy-start.7
  232.3 1.7 fusion.26
  234.0 0.0 copy-start.1
  234.0 0.0 copy-start.3
  234.0 12.7 %fusion.11 = f32[4096,1024]{1,0:T(8,128)} fusion(f32[256,512]{1,0:T(8,128)S(1)} %get-tuple-element.12, f32[256,512]{1,0:T(8,128)S(1)} %get-tuple-element.7, f32[256,512]{1,0:T(8,128)S(1)} %get-tuple-element.6, f32[256,4096]{1,0:T(8,128)} %get-tuple-element.14, f32[256,4096]{1,0:T(8,128)} %get-tuple-element.13), kind=kOutput, calls=%fused_computation.26 | convolution fusion | flops 4307025920 | bytes 26738688 | tf_op jit(solution)/shard_map/ka,kp->ap/dot_general | solution.py:28
  246.7 0.0 copy-done.7
  246.7 0.0 copy-done.1
  246.7 0.0 copy-done.3
  246.7 8.2 %fusion.19 = f32[4096,1024]{1,0:T(8,128)} fusion(f32[256,512]{1,0:T(8,128)S(1)} %get-tuple-element.12, f32[256,512]{1,0:T(8,128)S(1)} %get-tuple-element.7, f32[256,512]{1,0:T(8,128)S(1)} %get-tuple-element.6, f32[256,4096]{1,0:T(8,128)S(1)} %copy-done.3, f32[256,4096]{1,0:T(8,128)S(1)} %copy-done.1), kind=kOutput, calls=%fused_computation.39 | convolution fusion | flops 4307550208 | bytes 26738688 | tf_op jit(solution)/shard_map/ka,kp->ap/dot_general | solution.py:28
  254.9 19.3 %add_add_fusion = f32[4096,1024]{1,0:T(8,128)} fusion(f32[4096,1024]{1,0:T(8,128)} %fusion.19, f32[4096,1024]{1,0:T(8,128)} %fusion.11, f32[256,512]{1,0:T(8,128)S(1)} %get-tuple-element.12, f32[256,512]{1,0:T(8,128)S(1)} %get-tuple-element.7, f32[256,512]{1,0:T(8,128)S(1)} %get-tuple-element.6, f32[256,4096]{1,0:T(8,128)} %get-tuple-element.14, ...), kind=kOutput, calls=%fused_computation.2 | convolution fusion | flops 4318035968 | bytes 60293120 | tf_op jit(solution)/shard_map/ka,kp->ap/dot_general | solution.py:28
  274.1 6.9 %slice_bitcast_fusion.1 = (f32[1,4096,1,512]{3,1,2,0:T(8,128)S(1)}, f32[1,4096,1,512]{3,1,2,0:T(8,128)S(1)}) fusion(f32[4096,1024]{1,0:T(8,128)} %add_add_fusion), kind=kLoop, calls=%fused_computation.4 | loop fusion | bytes 33554432 | tf_op jit(solution)/shard_map/stack | solution.py:61
  281.0 2.5 fusion
  283.5 32.6 %copy.20 = bf16[2,4096,1,512]{3,0,2,1:T(2,128)(2,1)S(1)} copy(bf16[2,4096,1,512]{3,1,2,0:T(8,128)(2,1)S(1)} %fusion) | data formatting | bytes 16777216 | tf_op jit(solution)/shard_map/convert_element_type | solution.py:62
  316.2 102.3 %all_to_all.33 = bf16[2,4096,1,512]{3,0,2,1:T(2,128)(2,1)} all-to-all(bf16[2,4096,1,512]{3,0,2,1:T(2,128)(2,1)S(1)} %copy.20), channel_id=1, replica_groups=mesh['ang'=64,'pix'=2] {'ang'}, dimensions={1} | all-to-all | bytes 16777216 | tf_op jit(solution)/shard_map/all_to_all | solution.py:63
  418.4 8.0 %copy.21 = bf16[2,4096,1,512]{3,1,0,2:T(8,128)(2,1)} copy(bf16[2,4096,1,512]{3,0,2,1:T(2,128)(2,1)} %all_to_all.33) | data formatting | bytes 16777216 | tf_op jit(solution)/shard_map/all_to_all | solution.py:63
  426.4 11.5 %copy.22 = bf16[2,64,64,512]{3,2,1,0:T(8,128)(2,1)} copy(bf16[2,64,64,512]{3,1,2,0:T(8,128)(2,1)} %bitcast.18) | data formatting | bytes 16777216
  (1 shorter events, 0.0 us)
Async XLA Ops:
  12.1 11.9 %copy-start.6 = (s32[4096]{0:T(1024)S(1)}, s32[4096]{0:T(1024)}, u32[]{:S(2)}) copy-start(s32[4096]{0:T(1024)} %param.5) | copy-start | bytes 49156
  12.1 11.9 %copy-start.8 = (s32[256]{0:T(256)S(1)}, s32[256]{0:T(256)}, u32[]{:S(2)}) copy-start(s32[256]{0:T(256)} %param.6) | copy-start | bytes 3076
  12.1 114.6 %all-to-all-start = ((bf16[2,64,64,512]{3,1,0,2:T(8,128)(2,1)}), bf16[2,64,64,512]{3,1,0,2:T(8,128)(2,1)}, u32[]{:S(2)}, u32[]{:S(2)}) async-start(bf16[2,64,64,512]{3,1,0,2:T(8,128)(2,1)} %copy.18), calls=%async_computation | async-start | bytes 16777216 | tf_op jit(solution)/shard_map/all_to_all | solution.py:44
  134.6 7.5 %copy-start = (f32[256,4096]{1,0:T(8,128)S(1)}, f32[256,4096]{1,0:T(8,128)}, u32[]{:S(2)}) copy-start(f32[256,4096]{1,0:T(8,128)} %get-tuple-element.13) | copy-start | bytes 12582916
  134.6 9.0 %copy-start.2 = (f32[256,4096]{1,0:T(8,128)S(1)}, f32[256,4096]{1,0:T(8,128)}, u32[]{:S(2)}) copy-start(f32[256,4096]{1,0:T(8,128)} %get-tuple-element.14) | copy-start | bytes 12582916
  140.0 2.1 copy-start.5
  160.1 1.3 copy-start.4
  232.2 14.4 %copy-start.7 = (f32[256]{0:T(256)}, f32[256]{0:T(256)S(1)}, u32[]{:S(2)}) copy-start(f32[256]{0:T(256)S(1)} %add_sqrt_fusion) | copy-start | bytes 3076
  234.0 12.7 %copy-start.1 = (f32[256,4096]{1,0:T(8,128)S(1)}, f32[256,4096]{1,0:T(8,128)}, u32[]{:S(2)}) copy-start(f32[256,4096]{1,0:T(8,128)} %get-tuple-element.13) | copy-start | bytes 12582916
  234.0 12.7 %copy-start.3 = (f32[256,4096]{1,0:T(8,128)S(1)}, f32[256,4096]{1,0:T(8,128)}, u32[]{:S(2)}) copy-start(f32[256,4096]{1,0:T(8,128)} %get-tuple-element.14) | copy-start | bytes 12582916
where the time goes:
time: 438 us
  blocking collectives  173 us (39%)
  local copies, waits for them, and re-layouts  88.7 us (20%)
  waiting for transfers between devices  84.6 us (19%)
  matrix products  56.7 us (13%)
  other arithmetic  23.2 us (5%)
  starting transfers between devices  11.2 us (3%)
    all_to_all x1, blocking collectives, direct_path(): lax.all_to_all(update, 'ang', split_axis=1, concat_axis=2, tiled=True)  102 us
    all_to_all x1, waiting for transfers between devices, direct_path(): lax.all_to_all(grads, 'ang', split_axis=2, concat_axis=1, tiled=True)  84.6 us
    psum x1, blocking collectives, normalize(): totals = lax.psum(square_sums, ('ang', 'pix'))  70.5 us
    dot_general x5, matrix products, split_einsum(): jnp.einsum(form, left_piece, right_piece, preferred_element_type=jnp.floa...  56.7 us
    convert_element_type x1, local copies, waits for them, and re-layouts, direct_path(): update.astype(jnp.bfloat16).reshape(2, angle_count, row_local, col_count)  32.6 us
    unnamed x20, local copies, waits for them, and re-layouts  28 us
    cos x1, other arithmetic, phase_pair(): return (jnp.cos(radians), jnp.sin(radians))  18 us
    all_to_all x1, starting transfers between devices, direct_path(): lax.all_to_all(grads, 'ang', split_axis=2, concat_axis=1, tiled=True)  11.2 us
  transfers between devices with their start and end apart: 1, of which 1 were waited for; matrix products, arithmetic and copies ran while one was open for 4% of the time, Pallas kernels for 0%

commit v1 on v0

--- a/solution.py
+++ b/solution.py
@@ -32,7 +32,7 @@
 
 def normalize(coef_re, coef_im, weight, cell_count):
     square_sums = jnp.sum(weight[None, :] * (coef_re * coef_re + coef_im * coef_im), axis=1)
-    totals = lax.psum(square_sums, ("ang", "pix"))
+    totals = lax.psum(lax.psum(square_sums, "pix"), "ang")
     harmonic_rms = jnp.sqrt(totals / cell_count + 1e-06)
     factor = weight[None, :] / harmonic_rms[:, None]
     return (coef_re * factor, coef_im * factor, harmonic_rms)

time: 438 us -> 520 us (1.19)
  blocking collectives: 173 us -> 254 us
    psum x1 -> x2, blocking collectives: 70.5 us -> 149 us  [normalize(): totals = lax.psum(lax.psum(square_sums, 'pix'), 'ang')]
where the time goes in v1:
time: 520 us; the launch traced here: 519 us
  blocking collectives  254 us (49%)
  local copies, waits for them, and re-layouts  88.7 us (17%)
  waiting for transfers between devices  84.6 us (16%)
  matrix products  56.6 us (11%)
  other arithmetic  23.2 us (4%)
  starting transfers between devices  11.2 us (2%)
    psum x2, blocking collectives, normalize(): totals = lax.psum(lax.psum(square_sums, 'pix'), 'ang')  149 us
    all_to_all x1, blocking collectives, direct_path(): lax.all_to_all(update, 'ang', split_axis=1, concat_axis=2, tiled=True)  105 us
    all_to_all x1, waiting for transfers between devices, direct_path(): lax.all_to_all(grads, 'ang', split_axis=2, concat_axis=1, tiled=True)  84.6 us
    dot_general x5, matrix products, split_einsum(): jnp.einsum(form, left_piece, right_piece, preferred_element_type=jnp.floa...  56.6 us
    convert_element_type x1, local copies, waits for them, and re-layouts, direct_path(): update.astype(jnp.bfloat16).reshape(2, angle_count, row_local, col_count)  32.6 us
    unnamed x20, local copies, waits for them, and re-layouts  28 us
    cos x1, other arithmetic, phase_pair(): return (jnp.cos(radians), jnp.sin(radians))  18 us
    all_to_all x1, starting transfers between devices, direct_path(): lax.all_to_all(grads, 'ang', split_axis=2, concat_axis=1, tiled=True)  11.2 us
  transfers between devices with their start and end apart: 1, of which 1 were waited for; matrix products, arithmetic and copies ran while one was open for 4% of the time, Pallas kernels for 0%

profile of v1, /device:TPU:1, one launch (start us, length us, event | category | flops | bytes accessed | tf_op | source)
XLA Modules:
  0.0 519.1 jit_solution(16836612256237189103)
XLA Ops:
  0.6 11.5 %copy.18 = bf16[2,64,64,512]{3,1,0,2:T(8,128)(2,1)} copy(bf16[2,64,64,512]{3,2,1,0:T(8,128)(2,1)} %param.4) | data formatting | bytes 16777216 | tf_op args[0]
  12.1 0.0 copy-start.6
  12.1 0.0 copy-start.8
  12.1 11.2 %all-to-all-start = ((bf16[2,64,64,512]{3,1,0,2:T(8,128)(2,1)}), bf16[2,64,64,512]{3,1,0,2:T(8,128)(2,1)}, u32[]{:S(2)}, u32[]{:S(2)}) async-start(bf16[2,64,64,512]{3,1,0,2:T(8,128)(2,1)} %copy.18), calls=%async_computation | async-start | bytes 16777216 | tf_op jit(solution)/shard_map/all_to_all | solution.py:44
  23.3 0.7 dynamic-slice_convert_fusion
  24.1 0.0 copy-done.6
  24.1 0.0 copy-done.8
  24.1 18.0 %fusion.8 = (f32[256,4096]{1,0:T(8,128)}, f32[256,4096]{1,0:T(8,128)}) fusion(s32[4096]{0:T(1024)S(1)} %copy-done.6, s32[256]{0:T(256)S(1)} %copy-done.8), kind=kLoop, calls=%fused_computation.23 | loop fusion | flops 14680064 | bytes 8406016 | tf_op jit(solution)/shard_map/cos | solution.py:10
  42.1 84.6 %all-to-all-done = bf16[2,64,64,512]{3,1,0,2:T(8,128)(2,1)} async-done(((bf16[2,64,64,512]{3,1,0,2:T(8,128)(2,1)}), bf16[2,64,64,512]{3,1,0,2:T(8,128)(2,1)}, u32[]{:S(2)}, u32[]{:S(2)}) %all-to-all-start) | async-done | bytes 8388640 | tf_op jit(solution)/shard_map/all_to_all | solution.py:44
  126.7 7.9 %copy.24 = bf16[2,64,64,512]{3,1,2,0:T(8,128)(2,1)} copy(bf16[2,64,64,512]{3,1,0,2:T(8,128)(2,1)} %all-to-all-done) | data formatting | bytes 16777216 | tf_op jit(solution)/shard_map/all_to_all | solution.py:44
  134.6 0.0 copy-start
  134.6 0.0 copy-start.2
  134.6 5.4 %fusion.27 = (bf16[1,64,64,1,512]{4,2,1,3,0:T(8,128)(2,1)S(1)}, bf16[1,64,64,1,512]{4,2,1,3,0:T(8,128)(2,1)}) fusion(bf16[2,64,64,1,512]{4,2,1,3,0:T(8,128)(2,1)} %bitcast.17), kind=kLoop, calls=%fused_computation.41 | loop fusion | bytes 16777216 | tf_op jit(solution)/shard_map/slice | solution.py:51
  140.0 0.0 copy-start.5
  140.0 2.1 copy-done.5
  142.1 0.0 copy-done
  142.1 1.5 copy-done.2
  143.6 8.0 %fusion.2 = f32[512,1024]{1,0:T(8,128)} fusion(bf16[4096,512]{1,0:T(8,128)(2,1)} %bitcast.21, bf16[4096,512]{1,0:T(8,128)(2,1)S(1)} %bitcast.19, f32[256,4096]{1,0:T(8,128)S(1)} %copy-done.2, f32[256,4096]{1,0:T(8,128)S(1)} %copy-done), kind=kOutput, calls=%fused_computation.15 | convolution fusion | flops 4322230272 | bytes 18874368 | tf_op jit(solution)/shard_map/ka,ap->kp/dot_general | solution.py:28
  151.6 8.5 %fusion.9 = f32[512,1024]{1,0:T(8,128)S(1)} fusion(f32[512,1024]{1,0:T(8,128)} %fusion.2, bf16[4096,512]{1,0:T(8,128)(2,1)} %bitcast.22, bf16[4096,512]{1,0:T(8,128)(2,1)} %bitcast.20, f32[256,4096]{1,0:T(8,128)S(1)} %copy-done.2, f32[256,4096]{1,0:T(8,128)S(1)} %copy-done), kind=kOutput, calls=%fused_computation.24 | convolution fusion | flops 4320657408 | bytes 20971520 | tf_op jit(solution)/shard_map/ka,ap->kp/dot_general | solution.py:28
  160.1 0.0 copy-start.4
  160.2 1.3 copy-done.4
  161.5 0.2 multiply_reduce_fusion
  161.7 5.3 %psum.14 = f32[256]{0:T(256)S(1)} all-reduce(f32[256]{0:T(256)S(1)} %multiply_reduce_fusion), channel_id=1, replica_groups=mesh['ang'=64,'pix'=2] {'pix'}, use_global_device_ids=true, to_apply=%region_1.2 | all-reduce | flops 256 | bytes 2048 | tf_op jit(solution)/shard_map/psum | solution.py:35
  167.0 144.2 %psum.15 = f32[256]{0:T(256)S(1)} all-reduce(f32[256]{0:T(256)S(1)} %psum.14), channel_id=1, replica_groups=mesh['ang'=64,'pix'=2] {'ang'}, use_global_device_ids=true, to_apply=%region_2.3 | all-reduce | flops 256 | bytes 2048 | tf_op jit(solution)/shard_map/psum | solution.py:35
  311.2 0.0 copy-start.7
  311.2 1.7 fusion.26
  312.9 0.0 copy-start.1
  312.9 0.0 copy-start.3
  312.9 12.7 %fusion.11 = f32[4096,1024]{1,0:T(8,128)} fusion(f32[256,512]{1,0:T(8,128)S(1)} %get-tuple-element.12, f32[256,512]{1,0:T(8,128)S(1)} %get-tuple-element.7, f32[256,512]{1,0:T(8,128)S(1)} %get-tuple-element.6, f32[256,4096]{1,0:T(8,128)} %get-tuple-element.14, f32[256,4096]{1,0:T(8,128)} %get-tuple-element.13), kind=kOutput, calls=%fused_computation.26 | convolution fusion | flops 4307025920 | bytes 26738688 | tf_op jit(solution)/shard_map/ka,kp->ap/dot_general | solution.py:28
  325.6 0.0 copy-done.7
  325.6 0.0 copy-done.1
  325.6 0.0 copy-done.3
  325.6 8.2 %fusion.19 = f32[4096,1024]{1,0:T(8,128)} fusion(f32[256,512]{1,0:T(8,128)S(1)} %get-tuple-element.12, f32[256,512]{1,0:T(8,128)S(1)} %get-tuple-element.7, f32[256,512]{1,0:T(8,128)S(1)} %get-tuple-element.6, f32[256,4096]{1,0:T(8,128)S(1)} %copy-done.3, f32[256,4096]{1,0:T(8,128)S(1)} %copy-done.1), kind=kOutput, calls=%fused_computation.39 | convolution fusion | flops 4307550208 | bytes 26738688 | tf_op jit(solution)/shard_map/ka,kp->ap/dot_general | solution.py:28
  333.8 19.2 %add_add_fusion = f32[4096,1024]{1,0:T(8,128)} fusion(f32[4096,1024]{1,0:T(8,128)} %fusion.19, f32[4096,1024]{1,0:T(8,128)} %fusion.11, f32[256,512]{1,0:T(8,128)S(1)} %get-tuple-element.12, f32[256,512]{1,0:T(8,128)S(1)} %get-tuple-element.7, f32[256,512]{1,0:T(8,128)S(1)} %get-tuple-element.6, f32[256,4096]{1,0:T(8,128)} %get-tuple-element.14, ...), kind=kOutput, calls=%fused_computation.2 | convolution fusion | flops 4318035968 | bytes 60293120 | tf_op jit(solution)/shard_map/ka,kp->ap/dot_general | solution.py:28
  353.0 6.9 %slice_bitcast_fusion.1 = (f32[1,4096,1,512]{3,1,2,0:T(8,128)S(1)}, f32[1,4096,1,512]{3,1,2,0:T(8,128)S(1)}) fusion(f32[4096,1024]{1,0:T(8,128)} %add_add_fusion), kind=kLoop, calls=%fused_computation.4 | loop fusion | bytes 33554432 | tf_op jit(solution)/shard_map/stack | solution.py:61
  359.8 2.5 fusion
  362.3 32.6 %copy.20 = bf16[2,4096,1,512]{3,0,2,1:T(2,128)(2,1)S(1)} copy(bf16[2,4096,1,512]{3,1,2,0:T(8,128)(2,1)S(1)} %fusion) | data formatting | bytes 16777216 | tf_op jit(solution)/shard_map/convert_element_type | solution.py:62
  395.0 104.7 %all_to_all.33 = bf16[2,4096,1,512]{3,0,2,1:T(2,128)(2,1)} all-to-all(bf16[2,4096,1,512]{3,0,2,1:T(2,128)(2,1)S(1)} %copy.20), channel_id=1, replica_groups=mesh['ang'=64,'pix'=2] {'ang'}, dimensions={1} | all-to-all | bytes 16777216 | tf_op jit(solution)/shard_map/all_to_all | solution.py:63
  499.6 8.0 %copy.21 = bf16[2,4096,1,512]{3,1,0,2:T(8,128)(2,1)} copy(bf16[2,4096,1,512]{3,0,2,1:T(2,128)(2,1)} %all_to_all.33) | data formatting | bytes 16777216 | tf_op jit(solution)/shard_map/all_to_all | solution.py:63
  507.6 11.5 %copy.22 = bf16[2,64,64,512]{3,2,1,0:T(8,128)(2,1)} copy(bf16[2,64,64,512]{3,1,2,0:T(8,128)(2,1)} %bitcast.18) | data formatting | bytes 16777216
  (1 shorter events, 0.0 us)
Async XLA Ops:
  12.1 11.9 %copy-start.6 = (s32[4096]{0:T(1024)S(1)}, s32[4096]{0:T(1024)}, u32[]{:S(2)}) copy-start(s32[4096]{0:T(1024)} %param.5) | copy-start | bytes 49156
  12.1 11.9 %copy-start.8 = (s32[256]{0:T(256)S(1)}, s32[256]{0:T(256)}, u32[]{:S(2)}) copy-start(s32[256]{0:T(256)} %param.6) | copy-start | bytes 3076
  12.1 114.6 %all-to-all-start = ((bf16[2,64,64,512]{3,1,0,2:T(8,128)(2,1)}), bf16[2,64,64,512]{3,1,0,2:T(8,128)(2,1)}, u32[]{:S(2)}, u32[]{:S(2)}) async-start(bf16[2,64,64,512]{3,1,0,2:T(8,128)(2,1)} %copy.18), calls=%async_computation | async-start | bytes 16777216 | tf_op jit(solution)/shard_map/all_to_all | solution.py:44
  134.6 7.5 %copy-start = (f32[256,4096]{1,0:T(8,128)S(1)}, f32[256,4096]{1,0:T(8,128)}, u32[]{:S(2)}) copy-start(f32[256,4096]{1,0:T(8,128)} %get-tuple-element.13) | copy-start | bytes 12582916
  134.6 9.0 %copy-start.2 = (f32[256,4096]{1,0:T(8,128)S(1)}, f32[256,4096]{1,0:T(8,128)}, u32[]{:S(2)}) copy-start(f32[256,4096]{1,0:T(8,128)} %get-tuple-element.14) | copy-start | bytes 12582916
  140.0 2.1 copy-start.5
  160.1 1.3 copy-start.4
  311.2 14.4 %copy-start.7 = (f32[256]{0:T(256)}, f32[256]{0:T(256)S(1)}, u32[]{:S(2)}) copy-start(f32[256]{0:T(256)S(1)} %add_sqrt_fusion) | copy-start | bytes 3076
  312.9 12.7 %copy-start.1 = (f32[256,4096]{1,0:T(8,128)S(1)}, f32[256,4096]{1,0:T(8,128)}, u32[]{:S(2)}) copy-start(f32[256,4096]{1,0:T(8,128)} %get-tuple-element.13) | copy-start | bytes 12582916
  312.9 12.7 %copy-start.3 = (f32[256,4096]{1,0:T(8,128)S(1)}, f32[256,4096]{1,0:T(8,128)}, u32[]{:S(2)}) copy-start(f32[256,4096]{1,0:T(8,128)} %get-tuple-element.14) | copy-start | bytes 12582916
